TPU v7x, 512 devices: a whole 4x4x16 slice. The times are simulated.
512 devices in a mesh: grp: 4 (over y), seq: 32 (over z, core), mp: 4 (over x).
Axes of the slice: x: 4, y: 4, z: 16, core: 2. Of those that a mesh axis runs over, the one named last changes fastest.
Arguments:
- queries: bfloat16 [4, 4096, 2048], P('grp', 'seq', 'mp'), may hold values from -16 to 16
- d_out: bfloat16 [4, 4096, 2048], P('grp', 'seq', 'mp'), may hold values from -6 to 6
- neighbour_kv: bfloat16 [4, 256, 128, 2, 2048], P('grp', 'seq', None, None, 'mp'), may hold values from -16 to 16
- target: int32 [4, 256], P('grp', 'seq'), may hold values from -1 to 127, as said below
- bias: float32 [16, 191], P('mp'), may hold values from -6 to 6
Outputs:
- attended: bfloat16 [4, 4096, 2048], P('grp', 'seq', 'mp')
- d_query: bfloat16 [4, 4096, 2048], P('grp', 'seq', 'mp')
- d_kv: bfloat16 [4, 256, 128, 2, 2048], P('grp', 'seq', None, None, 'mp')
- d_bias: float32 [16, 191], P('mp')
Inputs may be any that keep to these rules, and one draw needn't show every extreme that they name: `target`: in each group every entry 0..127 stands in exactly one slot and -1 marks an empty slot. The slots of one index of seq hold at most 1 entries e with the same e // 4, and some index reaches that; some index of seq holds 8 entries.
All inputs are finite; a program needn't handle non-finite values.
Results may differ from a plain program's by a relative error of at most 0.011.
Values may be sent and summed in bfloat16 or wider, within the bound.
No kernel may reach another device: no remote copies, remote signals or barrier semaphores. Data moves between devices by JAX's collectives and lax.ppermute only.
A program may use at most 128 MiB of HBM per device.

v0:
```python
import jax
import jax.numpy as jnp
from jax import lax
from jax.sharding import PartitionSpec as P

STRETCH = 64
NB_LEN = 128


def passed_along(block, axis, distance):
    devices = range(lax.axis_size(axis))
    route = [(i - distance, i) for i in devices if i - distance in devices]
    return lax.ppermute(block, axis, route)


def bias_grid(lookup, row_count, col_count):
    head_num = lookup.shape[0]
    span = row_count + col_count
    padded = jnp.pad(lookup, ((0, 0), (0, 1)))
    flattened = jnp.tile(padded, (1, row_count))
    flattened = jnp.pad(flattened, ((0, 0), (0, row_count)))
    shaped = flattened.reshape(head_num, row_count, span + 1)[:, :, :col_count]
    return shaped[:, :, ::-1]


def bias_fold(grads):
    head_num, row_count, col_count = grads.shape
    turned = grads[:, :, ::-1]
    padded = jnp.pad(turned, ((0, 0), (0, 0), (0, row_count)))
    flattened = padded.reshape(head_num, row_count * (row_count + col_count))
    flattened = flattened[:, : row_count * (row_count + col_count - 1)]
    return jnp.sum(flattened.reshape(head_num, row_count, row_count + col_count - 1), axis=1)


def select_rows(picker, lookup):
    chosen = jnp.dot(
        picker.astype(lookup.dtype),
        lookup,
        preferred_element_type=jnp.float32,
        precision=lax.Precision.HIGHEST,
    )
    return chosen.astype(lookup.dtype)


def slot_places(target_row, owners, capacity, per_owner):
    is_used = target_row >= 0
    owner_of = jnp.where(is_used, target_row // per_owner, -1)
    positions = jnp.arange(target_row.shape[0])
    earlier = (
        (positions[None, :] < positions[:, None])
        & (owner_of[None, :] == owner_of[:, None])
        & is_used[None, :]
    )
    rank_of = jnp.sum(earlier.astype(jnp.int32), axis=1)
    match_owner = owner_of[None, :] == jnp.arange(owners)[:, None]
    match_rank = rank_of[None, :] == jnp.arange(capacity)[:, None]
    return match_owner[:, None, :] & match_rank[None, :, :] & is_used[None, None, :]


def local(queries, d_out, neighbour_kv, target, bias):
    tok_rows = queries.shape[1]
    width_dev = queries.shape[2]
    head_count = bias.shape[0]
    head_depth = width_dev // head_count
    stretch_count = tok_rows // STRETCH
    per_owner = 2 * stretch_count
    shard_count = lax.axis_size("seq")
    my_index = lax.axis_index("seq")
    group_size = min(shard_count, per_owner)
    capacity = (per_owner + group_size - 1) // group_size
    seq_stretches = min(2048, tok_rows * shard_count) // STRETCH
    scale_factor = head_depth ** (-0.5)
    bias_rows = bias_grid(bias, STRETCH, NB_LEN).transpose(1, 0, 2)
    q_rows = queries[0]
    g_rows = d_out[0]
    next_pair = passed_along(jnp.stack([q_rows[:STRETCH], g_rows[:STRETCH]]), "seq", -1)
    row_ids = jnp.arange(STRETCH)
    stretch_ids = my_index * stretch_count + jnp.arange(stretch_count)
    is_live = (row_ids[None, :] == 0) | ((stretch_ids[:, None] + 1) % seq_stretches != 0)
    live_rows = is_live.astype(jnp.float32)
    q_win = jnp.concatenate([q_rows, next_pair[0]])[STRETCH - 1 : STRETCH - 1 + tok_rows]
    q_win = q_win.reshape(stretch_count, STRETCH * width_dev)
    g_win = jnp.concatenate([g_rows, next_pair[1]])[STRETCH - 1 : STRETCH - 1 + tok_rows]
    g_win = g_win.reshape(stretch_count, STRETCH, width_dev) * is_live[:, :, None].astype(
        jnp.bfloat16
    )
    g_win = g_win.reshape(stretch_count, STRETCH * width_dev)
    my_targets = target[0]
    slot_count = my_targets.shape[0]
    send_map = slot_places(my_targets, shard_count, capacity, per_owner)
    id_buffer = jnp.sum(jnp.where(send_map, my_targets[None, None, :] + 1, 0), axis=2) - 1
    recv_ids = lax.all_to_all(id_buffer, "seq", split_axis=0, concat_axis=0, tiled=True)
    flat_ids = recv_ids.reshape(shard_count * capacity)
    has_entry = flat_ids >= 0
    local_entry = flat_ids - my_index * per_owner
    entry_pick = (local_entry[:, None] == jnp.arange(per_owner)[None, :]) & has_entry[:, None]
    stretch_pick = (local_entry[:, None] // 2 == jnp.arange(stretch_count)[None, :]) & has_entry[
        :, None
    ]
    back_pick = send_map.reshape(shard_count * capacity, slot_count)
    slot_pick = back_pick.T
    q_send = select_rows(stretch_pick, q_win).reshape(shard_count, capacity, STRETCH * width_dev)
    g_send = select_rows(stretch_pick, g_win).reshape(shard_count, capacity, STRETCH * width_dev)
    q_recv, g_recv = (
        lax.all_to_all(q_send, "seq", split_axis=0, concat_axis=0, tiled=True),
        lax.all_to_all(g_send, "seq", split_axis=0, concat_axis=0, tiled=True),
    )
    q_slots = select_rows(slot_pick, q_recv.reshape(shard_count * capacity, -1))
    q_slots = q_slots.reshape(slot_count, STRETCH, head_count, head_depth)
    stored = neighbour_kv[0]
    key_rows = stored[:, :, 0].reshape(slot_count, NB_LEN, head_count, head_depth)
    value_rows = stored[:, :, 1].reshape(slot_count, NB_LEN, head_count, head_depth)
    scores = jnp.einsum("sihd,sjhd->sihj", q_slots, key_rows, preferred_element_type=jnp.float32)
    scores = scores * scale_factor + bias_rows[None]
    peak_val = jnp.max(scores, axis=-1)
    weights = jnp.exp(scores - peak_val[..., None])
    row_total = jnp.sum(weights, axis=-1)
    partial_value = jnp.einsum(
        "sihj,sjhd->sihd",
        weights.astype(jnp.bfloat16),
        value_rows,
        preferred_element_type=jnp.float32,
    )
    part_send = select_rows(back_pick, partial_value.reshape(slot_count, -1)).reshape(
        shard_count, capacity, -1
    )
    peak_send = select_rows(back_pick, peak_val.reshape(slot_count, -1)).reshape(
        shard_count, capacity, -1
    )
    total_send = select_rows(back_pick, row_total.reshape(slot_count, -1)).reshape(
        shard_count, capacity, -1
    )
    part_recv, peak_recv, total_recv = (
        lax.all_to_all(part_send, "seq", split_axis=0, concat_axis=0, tiled=True),
        lax.all_to_all(peak_send, "seq", split_axis=0, concat_axis=0, tiled=True),
        lax.all_to_all(total_send, "seq", split_axis=0, concat_axis=0, tiled=True),
    )
    entry_back = entry_pick.T
    parts_own = select_rows(entry_back, part_recv.reshape(shard_count * capacity, -1))
    parts_own = parts_own.reshape(stretch_count, 2, STRETCH, head_count, head_depth)
    peaks_own = select_rows(entry_back, peak_recv.reshape(shard_count * capacity, -1))
    peaks_own = peaks_own.reshape(stretch_count, 2, STRETCH, head_count)
    totals_own = select_rows(entry_back, total_recv.reshape(shard_count * capacity, -1))
    totals_own = totals_own.reshape(stretch_count, 2, STRETCH, head_count)
    top_peak = jnp.max(peaks_own, axis=1)
    factor = jnp.exp(peaks_own - top_peak[:, None])
    denominator = jnp.sum(factor * totals_own, axis=1)
    combined = jnp.sum(factor[..., None] * parts_own, axis=1) / denominator[..., None]
    combined = combined * live_rows[:, :, None, None]
    att_win = combined.astype(jnp.bfloat16).reshape(tok_rows, width_dev)
    att_before = passed_along(att_win[tok_rows - STRETCH :], "seq", 1)
    log_total = top_peak + jnp.log(denominator)
    g_wide = g_win.reshape(stretch_count, STRETCH, head_count, head_depth).astype(jnp.float32)
    inner_dot = jnp.sum(g_wide * combined, axis=-1)
    row_stats = jnp.repeat(jnp.stack([log_total, inner_dot], axis=1), 2, axis=0)
    stats_send = select_rows(entry_pick, row_stats.reshape(per_owner, -1)).reshape(
        shard_count, capacity, -1
    )
    stats_recv = lax.all_to_all(stats_send, "seq", split_axis=0, concat_axis=0, tiled=True)
    g_slots = select_rows(slot_pick, g_recv.reshape(shard_count * capacity, -1))
    g_slots = g_slots.reshape(slot_count, STRETCH, head_count, head_depth)
    stats_slots = select_rows(slot_pick, stats_recv.reshape(shard_count * capacity, -1))
    stats_slots = stats_slots.reshape(slot_count, 2, STRETCH, head_count)
    prob_full = jnp.exp(scores - stats_slots[:, 0][..., None])
    prob_low = prob_full.astype(jnp.bfloat16)
    grad_values = jnp.einsum(
        "sihj,sihd->sjhd", prob_low, g_slots, preferred_element_type=jnp.float32
    )
    grad_prob = jnp.einsum(
        "sihd,sjhd->sihj", g_slots, value_rows, preferred_element_type=jnp.float32
    )
    grad_scores = prob_full * (grad_prob - stats_slots[:, 1][..., None])
    scores_low = grad_scores.astype(jnp.bfloat16)
    grad_rows = (
        jnp.einsum("sihj,sjhd->sihd", scores_low, key_rows, preferred_element_type=jnp.float32)
        * scale_factor
    )
    grad_keys = (
        jnp.einsum("sihj,sihd->sjhd", scores_low, q_slots, preferred_element_type=jnp.float32)
        * scale_factor
    )
    d_kv = jnp.stack(
        [
            grad_keys.reshape(slot_count, NB_LEN, width_dev),
            grad_values.reshape(slot_count, NB_LEN, width_dev),
        ],
        axis=2,
    ).astype(jnp.bfloat16)
    bias_part = bias_fold(jnp.sum(grad_scores, axis=0).transpose(1, 0, 2))
    rows_send = select_rows(back_pick, grad_rows.reshape(slot_count, -1)).reshape(
        shard_count, capacity, -1
    )
    rows_recv = lax.all_to_all(rows_send, "seq", split_axis=0, concat_axis=0, tiled=True)
    grad_entries = select_rows(entry_back, rows_recv.reshape(shard_count * capacity, -1))
    grad_entries = grad_entries.reshape(stretch_count, 2, STRETCH * width_dev)
    grad_win = (
        (grad_entries[:, 0] + grad_entries[:, 1]).astype(jnp.bfloat16).reshape(tok_rows, width_dev)
    )
    grad_before = passed_along(grad_win[tok_rows - STRETCH :], "seq", 1)
    attended = jnp.concatenate([att_before[1:], att_win[: tok_rows - STRETCH + 1]])
    d_query = jnp.concatenate([grad_before[1:], grad_win[: tok_rows - STRETCH + 1]])
    raw_sum = lax.psum(bias_part, ("grp", "seq"))
    squares = lax.psum(jnp.sum(raw_sum * raw_sum), "mp")
    d_bias = raw_sum * jnp.minimum(1.0, 1.0 / jnp.sqrt(squares + 1e-12))
    return (attended[None], d_query[None], d_kv[None], d_bias)


def solution(mesh):
    in_specs = (
        P("grp", "seq", "mp"),
        P("grp", "seq", "mp"),
        P("grp", "seq", None, None, "mp"),
        P("grp", "seq"),
        P("mp", None),
    )
    out_specs = (
        P("grp", "seq", "mp"),
        P("grp", "seq", "mp"),
        P("grp", "seq", None, None, "mp"),
        P("mp", None),
    )
    return jax.shard_map(local, mesh=mesh, in_specs=in_specs, out_specs=out_specs, check_vma=False)
```

profile of v0, /device:TPU:1, one launch (start us, length us, event | category | flops | bytes accessed | tf_op | source)
XLA Modules:
  0.0 1025.3 jit_solution(9001594490378168722)
XLA Ops:
  3.6 0.7 copy.156
  4.3 16.7 %all-to-all-start = ((s32[32,1,1]{2,1,0:T(1,128)}), s32[32,1,1]{2,1,0:T(1,128)S(1)}, u32[]{:S(2)}, u32[]{:S(2)}) async-start(s32[32,1,1]{2,1,0:T(1,128)} %copy.156), calls=%async_computation | async-start | bytes 32768 | tf_op jit(solution)/shard_map/all_to_all | solution.py:92
  21.0 0.8 slice.70
  21.9 0.8 slice.69
  22.7 2.1 collective-permute-start
  24.9 7.8 all-to-all-done
  34.1 0.9 pad_maximum_fusion.2
  35.1 0.7 fusion
  36.4 2.9 reduce.9
  39.3 4.5 reshape.685
  43.8 6.9 all-to-all-start.1
  51.2 2.1 fusion.1
  53.3 4.5 reduce.10
  57.8 4.5 reshape.687
  62.3 87.0 %all-to-all-done.1 = bf16[32,2,16384]{2,1,0:T(2,128)(2,1)S(1)} async-done(((bf16[32,2,16384]{2,1,0:T(2,128)(2,1)}), bf16[32,2,16384]{2,1,0:T(2,128)(2,1)S(1)}, u32[]{:S(2)}, u32[]{:S(2)}) %all-to-all-start.1) | async-done | bytes 2097184 | tf_op jit(solution)/shard_map/all_to_all | solution.py:105
  149.3 5.2 all-to-all-start.6
  154.5 6.2 copy.158
  161.5 2.7 fusion.78
  164.1 10.5 %reshape.686 = bf16[32,1,32768]{2,1,0:T(2,128)(2,1)} reshape(bf16[32,2,16384]{2,1,0:T(2,128)(2,1)} %copy-done) | data formatting | bytes 4194304
  174.6 4.5 convolution_convert_fusion.3
  179.1 0.8 copy-done.4
  179.9 1.9 fusion.79
  182.7 1.8 convolution_bitcast_fusion.3
  184.6 69.2 %all-to-all-done.6 = bf16[32,2,16384]{2,1,0:T(2,128)(2,1)} async-done(((bf16[32,2,16384]{2,1,0:T(2,128)(2,1)}), bf16[32,2,16384]{2,1,0:T(2,128)(2,1)}, u32[]{:S(2)}, u32[]{:S(2)}) %all-to-all-start.6) | async-done | bytes 2097184 | tf_op jit(solution)/shard_map/all_to_all | solution.py:106
  253.8 6.3 all-to-all-start.2
  260.7 2.9 copy.167
  263.6 2.7 reshape.655
  267.3 5.0 all-to-all-done.2
  272.3 7.3 all-to-all-start.4
  279.6 3.1 convolution_bitcast_fusion.1
  282.7 6.3 copy.168
  289.0 2.7 all-to-all-done.4
  291.7 9.9 all-to-all-start.3
  301.7 10.5 %reshape.688 = bf16[32,1,32768]{2,1,0:T(2,128)(2,1)} reshape(bf16[32,2,16384]{2,1,0:T(2,128)(2,1)} %all-to-all-done.6) | data formatting | bytes 4194304
  313.4 171.4 %all-to-all-done.3 = f32[32,1,32768]{2,1,0:T(1,128)} async-done(((f32[32,1,32768]{2,1,0:T(1,128)}), f32[32,1,32768]{2,1,0:T(1,128)}, u32[]{:S(2)}, u32[]{:S(2)}) %all-to-all-start.3) | async-done | bytes 4194336 | tf_op jit(solution)/shard_map/all_to_all | solution.py:134
  484.7 6.6 copy.249
  491.3 6.0 dot_general.86
  497.4 6.8 fusion.20
  504.1 1.1 multiply_reduce_fusion
  505.9 0.7 copy.177
  506.6 10.9 %all-to-all-start.5 = ((f32[32,1,512]{2,1,0:T(1,128)}), f32[32,1,512]{2,1,0:T(1,128)S(1)}, u32[]{:S(2)}, u32[]{:S(2)}) async-start(f32[32,1,512]{2,1,0:T(1,128)} %copy.177), calls=%async_computation.5 | async-start | bytes 131072 | tf_op jit(solution)/shard_map/all_to_all | solution.py:159
  517.5 4.5 convolution_convert_fusion.2
  522.0 8.5 all-to-all-done.5
  531.1 0.8 fusion.81
  531.9 0.8 copy-done.3
  532.7 2.0 fusion.12
  534.8 0.7 copy.186
  535.5 1.5 reshape.668
  537.0 3.1 convolution_bitcast_fusion
  540.1 6.3 copy.187
  546.4 6.1 all-to-all-start.7
  552.9 3.7 collective-permute-start.1
  556.7 169.2 %collective-permute-done.1 = bf16[64,512]{1,0:T(8,128)(2,1)S(1)} collective-permute-done((bf16[64,512]{1,0:T(8,128)(2,1)S(1)}, bf16[64,512]{1,0:T(8,128)(2,1)S(1)}, u32[]{:S(2)}, u32[]{:S(2)}) %collective-permute-start.1) | collective-permute-done | bytes 65568 | tf_op jit(solution)/shard_map/ppermute | solution.py:13
  726.5 256.5 %psum.14 = f32[4,191]{1,0:T(4,128)S(1)} all-reduce(f32[4,191]{1,0:T(4,128)S(1)} %reduce_sum.88), channel_id=1, replica_groups=mesh['grp'=4,'seq'=32,'mp'=4] {'grp','seq'}, use_global_device_ids=true, to_apply=%region_10.11 | all-reduce | flops 764 | bytes 6112 | tf_op jit(solution)/shard_map/psum | solution.py:202
  984.3 9.1 psum.15
  993.4 1.8 convolution_convert_fusion.4
  995.2 4.6 copy.191
  999.8 1.8 multiply_convert_fusion
  1001.6 3.8 copy.190
  1006.1 6.7 pad_maximum_fusion
  1012.8 6.0 fusion.2
  1018.8 1.0 fusion.76
  1020.3 1.9 collective-permute-start.2
  1022.9 1.6 collective-permute-done.2
  (99 shorter events, 15.2 us)
Async XLA Ops:
  4.3 28.5 %all-to-all-start = ((s32[32,1,1]{2,1,0:T(1,128)}), s32[32,1,1]{2,1,0:T(1,128)S(1)}, u32[]{:S(2)}, u32[]{:S(2)}) async-start(s32[32,1,1]{2,1,0:T(1,128)} %copy.156), calls=%async_computation | async-start | bytes 32768 | tf_op jit(solution)/shard_map/all_to_all | solution.py:92
  22.7 11.4 %collective-permute-start = (bf16[2,64,512]{2,1,0:T(8,128)(2,1)S(1)}, bf16[2,64,512]{2,1,0:T(8,128)(2,1)S(1)}, u32[]{:S(2)}, u32[]{:S(2)}) collective-permute-start(bf16[2,64,512]{2,1,0:T(8,128)(2,1)S(1)} %pad_maximum_fusion.3), channel_id=1, source_target_pairs={{4,0},{8,4},{12,8},{16,12},{20,16},{24,20},{28,24},{32,28},{36,32}... | collective-permute-start | bytes 393224 | tf_op jit(solution)/shard_map/ppermute | solution.py:13
  39.3 11.7 %copy-start.5 = (bf16[1,128,512]{2,1,0:T(8,128)(2,1)S(1)}, bf16[1,128,512]{2,1,0:T(8,128)(2,1)}, u32[]{:S(2)}) copy-start(bf16[1,128,512]{2,1,0:T(8,128)(2,1)} %param.6) | copy-start | bytes 393220
  43.8 105.5 %all-to-all-start.1 = ((bf16[32,2,16384]{2,1,0:T(2,128)(2,1)}), bf16[32,2,16384]{2,1,0:T(2,128)(2,1)S(1)}, u32[]{:S(2)}, u32[]{:S(2)}) async-start(bf16[32,2,16384]{2,1,0:T(2,128)(2,1)} %reshape.685), calls=%async_computation.1 | async-start | bytes 4194304 | tf_op jit(solution)/shard_map/all_to_all | solution.py:105
  62.3 98.4 %copy-start.7 = (f32[4,191]{1,0:T(4,128)S(1)}, f32[4,191]{1,0:T(4,128)}, u32[]{:S(2)}) copy-start(f32[4,191]{1,0:T(4,128)} %param.9) | copy-start | bytes 9172
  149.3 11.4 %copy-start = (bf16[32,2,16384]{2,1,0:T(2,128)(2,1)}, bf16[32,2,16384]{2,1,0:T(2,128)(2,1)S(1)}, u32[]{:S(2)}) copy-start(bf16[32,2,16384]{2,1,0:T(2,128)(2,1)S(1)} %all-to-all-done.1) | copy-start | bytes 6291460
  149.3 104.5 %all-to-all-start.6 = ((bf16[32,2,16384]{2,1,0:T(2,128)(2,1)}), bf16[32,2,16384]{2,1,0:T(2,128)(2,1)}, u32[]{:S(2)}, u32[]{:S(2)}) async-start(bf16[32,2,16384]{2,1,0:T(2,128)(2,1)} %reshape.687), calls=%async_computation.6 | async-start | bytes 4194304 | tf_op jit(solution)/shard_map/all_to_all | solution.py:106
  179.1 0.8 copy-start.4
  253.8 18.5 %all-to-all-start.2 = ((f32[32,1,256]{2,1,0:T(1,128)}), f32[32,1,256]{2,1,0:T(1,128)S(1)}, u32[]{:S(2)}, u32[]{:S(2)}) async-start(f32[32,1,256]{2,1,0:T(1,128)} %copy.162), calls=%async_computation.2 | async-start | bytes 65536 | tf_op jit(solution)/shard_map/all_to_all | solution.py:135
  272.3 19.4 %all-to-all-start.4 = ((f32[32,1,256]{2,1,0:T(1,128)}), f32[32,1,256]{2,1,0:T(1,128)S(1)}, u32[]{:S(2)}, u32[]{:S(2)}) async-start(f32[32,1,256]{2,1,0:T(1,128)} %copy.171), calls=%async_computation.4 | async-start | bytes 65536 | tf_op jit(solution)/shard_map/all_to_all | solution.py:136
  291.7 193.0 %all-to-all-start.3 = ((f32[32,1,32768]{2,1,0:T(1,128)}), f32[32,1,32768]{2,1,0:T(1,128)}, u32[]{:S(2)}, u32[]{:S(2)}) async-start(f32[32,1,32768]{2,1,0:T(1,128)} %copy.168), calls=%async_computation.3 | async-start | bytes 8388608 | tf_op jit(solution)/shard_map/all_to_all | solution.py:134
  506.6 23.9 %all-to-all-start.5 = ((f32[32,1,512]{2,1,0:T(1,128)}), f32[32,1,512]{2,1,0:T(1,128)S(1)}, u32[]{:S(2)}, u32[]{:S(2)}) async-start(f32[32,1,512]{2,1,0:T(1,128)} %copy.177), calls=%async_computation.5 | async-start | bytes 131072 | tf_op jit(solution)/shard_map/all_to_all | solution.py:159
  522.0 13.5 %copy-start.1 = (bf16[8,32768]{1,0:T(8,128)(2,1)}, bf16[8,32768]{1,0:T(8,128)(2,1)S(1)}, u32[]{:S(2)}) copy-start(bf16[8,32768]{1,0:T(8,128)(2,1)S(1)} %convolution_convert_fusion.2) | copy-start | bytes 1572868
  531.9 0.8 copy-start.3
  546.4 6.4 copy-start.6
  546.4 447.1 %copy-start.2 = (bf16[8,32768]{1,0:T(8,128)(2,1)S(1)}, bf16[8,32768]{1,0:T(8,128)(2,1)}, u32[]{:S(2)}) copy-start(bf16[8,32768]{1,0:T(8,128)(2,1)} %copy-done.1) | copy-start | bytes 1572868
  546.4 466.4 %all-to-all-start.7 = ((f32[32,1,32768]{2,1,0:T(1,128)}), f32[32,1,32768]{2,1,0:T(1,128)}, u32[]{:S(2)}, u32[]{:S(2)}) async-start(f32[32,1,32768]{2,1,0:T(1,128)} %copy.187), calls=%async_computation.7 | async-start | bytes 8388608 | tf_op jit(solution)/shard_map/all_to_all | solution.py:193
  552.9 173.0 %collective-permute-start.1 = (bf16[64,512]{1,0:T(8,128)(2,1)S(1)}, bf16[64,512]{1,0:T(8,128)(2,1)S(1)}, u32[]{:S(2)}, u32[]{:S(2)}) collective-permute-start(bf16[64,512]{1,0:T(8,128)(2,1)S(1)} %bitcast.224), channel_id=1, source_target_pairs={{0,4},{4,8},{8,12},{12,16},{16,20},{20,24},{24,28},{28,32},{32,36}... | collective-permute-start | bytes 196616 | tf_op jit(solution)/shard_map/ppermute | solution.py:13
  1020.3 4.2 collective-permute-start.2
where the time goes:
time: 1040 us; the launch traced here: 1030 us
  waiting for transfers between devices  522 us (50%)
  blocking collectives  266 us (26%)
  local copies, waits for them, and re-layouts  90.5 us (9%)
  starting transfers between devices  77.1 us (7%)
  matrix products  42.5 us (4%)
  other arithmetic  25.1 us (2%)
    psum x1, blocking collectives, local(): raw_sum = lax.psum(bias_part, ('grp', 'seq'))  257 us
    all_to_all x1, waiting for transfers between devices, local(): lax.all_to_all(part_send, 'seq', split_axis=0, concat_axis=0, tiled=True)  171 us
    ppermute x3, waiting for transfers between devices, passed_along(): return lax.ppermute(block, axis, route)  171 us
    all_to_all x1, waiting for transfers between devices, local(): lax.all_to_all(q_send, 'seq', split_axis=0, concat_axis=0, tiled=True)  87 us
    all_to_all x1, waiting for transfers between devices, local(): lax.all_to_all(g_send, 'seq', split_axis=0, concat_axis=0, tiled=True)  69.2 us
    unnamed x26, local copies, waits for them, and re-layouts  44.6 us
    dot_general x14, matrix products, select_rows(): jnp.dot(picker.astype(lookup.dtype), lookup, preferred_element_type=jnp.f...  32.4 us
  transfers between devices with their start and end apart: 11, of which 9 were waited for; matrix products, arithmetic and copies ran while one was open for 10% of the time, Pallas kernels for 0%

commit v1 on v0

--- a/solution.py
+++ b/solution.py
@@ -199,7 +199,7 @@
     grad_before = passed_along(grad_win[tok_rows - STRETCH :], "seq", 1)
     attended = jnp.concatenate([att_before[1:], att_win[: tok_rows - STRETCH + 1]])
     d_query = jnp.concatenate([grad_before[1:], grad_win[: tok_rows - STRETCH + 1]])
-    raw_sum = lax.psum(bias_part, ("grp", "seq"))
+    raw_sum = lax.psum(lax.psum(bias_part, "seq"), "grp")
     squares = lax.psum(jnp.sum(raw_sum * raw_sum), "mp")
     d_bias = raw_sum * jnp.minimum(1.0, 1.0 / jnp.sqrt(squares + 1e-12))
     return (attended[None], d_query[None], d_kv[None], d_bias)

time: 1040 us -> 846 us (0.81)
  blocking collectives: 266 us -> 73 us
    psum x1 -> x2, blocking collectives: 257 us -> 63.9 us  [local(): raw_sum = lax.psum(lax.psum(bias_part, 'seq'), 'grp')]
  transfers between devices with their start and end apart: 11 -> 11, of which waited for: 9 -> 9; matrix products, arithmetic and copies ran while one was open for 10% -> 12% of each run, Pallas kernels for 0% -> 0%
where the time goes in v1:
time: 846 us; the launch traced here: 835 us
  waiting for transfers between devices  522 us (62%)
  local copies, waits for them, and re-layouts  90.5 us (11%)
  starting transfers between devices  79.4 us (9%)
  blocking collectives  73 us (9%)
  matrix products  42.5 us (5%)
  other arithmetic  25.1 us (3%)
    all_to_all x1, waiting for transfers between devices, local(): lax.all_to_all(part_send, 'seq', split_axis=0, concat_axis=0, tiled=True)  171 us
    ppermute x3, waiting for transfers between devices, passed_along(): return lax.ppermute(block, axis, route)  170 us
    all_to_all x1, waiting for transfers between devices, local(): lax.all_to_all(q_send, 'seq', split_axis=0, concat_axis=0, tiled=True)  87 us
    all_to_all x1, waiting for transfers between devices, local(): lax.all_to_all(g_send, 'seq', split_axis=0, concat_axis=0, tiled=True)  69.2 us
    psum x2, blocking collectives, local(): raw_sum = lax.psum(lax.psum(bias_part, 'seq'), 'grp')  63.9 us
    unnamed x26, local copies, waits for them, and re-layouts  44.6 us
    dot_general x14, matrix products, select_rows(): jnp.dot(picker.astype(lookup.dtype), lookup, preferred_element_type=jnp.f...  32.4 us
  transfers between devices with their start and end apart: 11, of which 9 were waited for; matrix products, arithmetic and copies ran while one was open for 12% of the time, Pallas kernels for 0%

profile of v1, /device:TPU:1, one launch (start us, length us, event | category | flops | bytes accessed | tf_op | source)
XLA Modules:
  0.0 834.7 jit_solution(18104832837315478708)
XLA Ops:
  3.6 0.7 copy.156
  4.3 16.7 %all-to-all-start = ((s32[32,1,1]{2,1,0:T(1,128)}), s32[32,1,1]{2,1,0:T(1,128)S(1)}, u32[]{:S(2)}, u32[]{:S(2)}) async-start(s32[32,1,1]{2,1,0:T(1,128)} %copy.156), calls=%async_computation | async-start | bytes 32768 | tf_op jit(solution)/shard_map/all_to_all | solution.py:92
  21.0 0.8 slice.70
  21.9 0.8 slice.69
  22.7 2.1 collective-permute-start
  24.9 7.8 all-to-all-done
  34.1 0.9 pad_maximum_fusion.2
  35.1 0.7 fusion
  36.4 2.9 reduce.9
  39.3 4.5 reshape.685
  43.8 6.9 all-to-all-start.1
  51.2 2.1 fusion.1
  53.3 4.5 reduce.10
  57.8 4.5 reshape.687
  62.3 87.0 %all-to-all-done.1 = bf16[32,2,16384]{2,1,0:T(2,128)(2,1)S(1)} async-done(((bf16[32,2,16384]{2,1,0:T(2,128)(2,1)}), bf16[32,2,16384]{2,1,0:T(2,128)(2,1)S(1)}, u32[]{:S(2)}, u32[]{:S(2)}) %all-to-all-start.1) | async-done | bytes 2097184 | tf_op jit(solution)/shard_map/all_to_all | solution.py:105
  149.3 5.2 all-to-all-start.6
  154.5 6.2 copy.158
  161.5 2.7 fusion.78
  164.1 10.5 %reshape.686 = bf16[32,1,32768]{2,1,0:T(2,128)(2,1)} reshape(bf16[32,2,16384]{2,1,0:T(2,128)(2,1)} %copy-done) | data formatting | bytes 4194304
  174.6 4.5 convolution_convert_fusion.3
  179.1 0.8 copy-done.4
  179.9 1.9 fusion.79
  182.7 1.8 convolution_bitcast_fusion.3
  184.6 69.2 %all-to-all-done.6 = bf16[32,2,16384]{2,1,0:T(2,128)(2,1)} async-done(((bf16[32,2,16384]{2,1,0:T(2,128)(2,1)}), bf16[32,2,16384]{2,1,0:T(2,128)(2,1)}, u32[]{:S(2)}, u32[]{:S(2)}) %all-to-all-start.6) | async-done | bytes 2097184 | tf_op jit(solution)/shard_map/all_to_all | solution.py:106
  253.8 6.3 all-to-all-start.2
  260.7 2.9 copy.167
  263.6 2.7 reshape.655
  267.3 5.0 all-to-all-done.2
  272.3 7.3 all-to-all-start.4
  279.6 3.1 convolution_bitcast_fusion.1
  282.7 6.3 copy.168
  289.0 2.7 all-to-all-done.4
  291.7 9.9 %all-to-all-start.3 = ((f32[32,1,32768]{2,1,0:T(1,128)}), f32[32,1,32768]{2,1,0:T(1,128)}, u32[]{:S(2)}, u32[]{:S(2)}) async-start(f32[32,1,32768]{2,1,0:T(1,128)} %copy.168), calls=%async_computation.3 | async-start | bytes 8388608 | tf_op jit(solution)/shard_map/all_to_all | solution.py:134
  301.7 10.5 %reshape.688 = bf16[32,1,32768]{2,1,0:T(2,128)(2,1)} reshape(bf16[32,2,16384]{2,1,0:T(2,128)(2,1)} %all-to-all-done.6) | data formatting | bytes 4194304
  313.4 171.4 %all-to-all-done.3 = f32[32,1,32768]{2,1,0:T(1,128)} async-done(((f32[32,1,32768]{2,1,0:T(1,128)}), f32[32,1,32768]{2,1,0:T(1,128)}, u32[]{:S(2)}, u32[]{:S(2)}) %all-to-all-start.3) | async-done | bytes 4194336 | tf_op jit(solution)/shard_map/all_to_all | solution.py:134
  484.7 6.6 copy.249
  491.3 6.0 dot_general.86
  497.4 6.8 fusion.20
  504.1 1.1 multiply_reduce_fusion
  505.9 0.7 copy.177
  506.6 10.9 %all-to-all-start.5 = ((f32[32,1,512]{2,1,0:T(1,128)}), f32[32,1,512]{2,1,0:T(1,128)S(1)}, u32[]{:S(2)}, u32[]{:S(2)}) async-start(f32[32,1,512]{2,1,0:T(1,128)} %copy.177), calls=%async_computation.5 | async-start | bytes 131072 | tf_op jit(solution)/shard_map/all_to_all | solution.py:159
  517.5 4.5 convolution_convert_fusion.2
  522.0 8.5 %all-to-all-done.5 = f32[32,1,512]{2,1,0:T(1,128)S(1)} async-done(((f32[32,1,512]{2,1,0:T(1,128)}), f32[32,1,512]{2,1,0:T(1,128)S(1)}, u32[]{:S(2)}, u32[]{:S(2)}) %all-to-all-start.5) | async-done | bytes 65568 | tf_op jit(solution)/shard_map/all_to_all | solution.py:159
  531.1 0.8 fusion.81
  531.9 0.8 copy-done.3
  532.7 2.0 fusion.12
  535.5 1.5 reshape.668
  537.0 3.1 convolution_bitcast_fusion
  540.1 6.3 copy.187
  546.4 6.1 all-to-all-start.7
  552.9 3.7 collective-permute-start.1
  556.7 169.2 %collective-permute-done.1 = bf16[64,512]{1,0:T(8,128)(2,1)S(1)} collective-permute-done((bf16[64,512]{1,0:T(8,128)(2,1)S(1)}, bf16[64,512]{1,0:T(8,128)(2,1)S(1)}, u32[]{:S(2)}, u32[]{:S(2)}) %collective-permute-start.1) | collective-permute-done | bytes 65568 | tf_op jit(solution)/shard_map/ppermute | solution.py:13
  726.5 55.2 %psum.21 = f32[4,191]{1,0:T(4,128)S(1)} all-reduce(f32[4,191]{1,0:T(4,128)S(1)} %reduce_sum.88), channel_id=1, replica_groups=mesh['grp'=4,'seq'=32,'mp'=4] {'seq'}, use_global_device_ids=true, to_apply=%region_10.11 | all-reduce | flops 764 | bytes 6112 | tf_op jit(solution)/shard_map/psum | solution.py:202
  781.7 8.7 %psum.22 = f32[4,191]{1,0:T(4,128)S(1)} all-reduce(f32[4,191]{1,0:T(4,128)S(1)} %psum.21), channel_id=1, replica_groups=mesh['grp'=4,'seq'=32,'mp'=4] {'grp'}, use_global_device_ids=true, to_apply=%region_11.12 | all-reduce | flops 764 | bytes 6112 | tf_op jit(solution)/shard_map/psum | solution.py:202
  791.7 9.1 %psum.23 = f32[]{:T(128)} all-reduce(f32[]{:T(128)} %multiply_reduce_fusion.1), channel_id=1, replica_groups=mesh['grp'=4,'seq'=32,'mp'=4] {'mp'}, use_global_device_ids=true, to_apply=%region_13.14 | all-reduce | flops 1 | bytes 8 | tf_op jit(solution)/shard_map/psum | solution.py:203
  800.8 1.8 convolution_convert_fusion.4
  802.6 4.6 copy.191
  807.2 1.8 multiply_convert_fusion
  809.0 3.8 copy.190
  813.5 6.7 pad_maximum_fusion
  820.1 6.0 fusion.2
  826.2 1.0 fusion.76
  827.6 4.3 collective-permute-start.2
  832.6 1.3 collective-permute-done.2
  (100 shorter events, 15.9 us)
Async XLA Ops:
  4.3 28.5 %all-to-all-start = ((s32[32,1,1]{2,1,0:T(1,128)}), s32[32,1,1]{2,1,0:T(1,128)S(1)}, u32[]{:S(2)}, u32[]{:S(2)}) async-start(s32[32,1,1]{2,1,0:T(1,128)} %copy.156), calls=%async_computation | async-start | bytes 32768 | tf_op jit(solution)/shard_map/all_to_all | solution.py:92
  22.7 11.4 %collective-permute-start = (bf16[2,64,512]{2,1,0:T(8,128)(2,1)S(1)}, bf16[2,64,512]{2,1,0:T(8,128)(2,1)S(1)}, u32[]{:S(2)}, u32[]{:S(2)}) collective-permute-start(bf16[2,64,512]{2,1,0:T(8,128)(2,1)S(1)} %pad_maximum_fusion.3), channel_id=1, source_target_pairs={{4,0},{8,4},{12,8},{16,12},{20,16},{24,20},{28,24},{32,28},{36,32}... | collective-permute-start | bytes 393224 | tf_op jit(solution)/shard_map/ppermute | solution.py:13
  39.3 11.7 %copy-start.5 = (bf16[1,128,512]{2,1,0:T(8,128)(2,1)S(1)}, bf16[1,128,512]{2,1,0:T(8,128)(2,1)}, u32[]{:S(2)}) copy-start(bf16[1,128,512]{2,1,0:T(8,128)(2,1)} %param.6) | copy-start | bytes 393220
  43.8 105.5 %all-to-all-start.1 = ((bf16[32,2,16384]{2,1,0:T(2,128)(2,1)}), bf16[32,2,16384]{2,1,0:T(2,128)(2,1)S(1)}, u32[]{:S(2)}, u32[]{:S(2)}) async-start(bf16[32,2,16384]{2,1,0:T(2,128)(2,1)} %reshape.685), calls=%async_computation.1 | async-start | bytes 4194304 | tf_op jit(solution)/shard_map/all_to_all | solution.py:105
  62.3 98.4 %copy-start.7 = (f32[4,191]{1,0:T(4,128)S(1)}, f32[4,191]{1,0:T(4,128)}, u32[]{:S(2)}) copy-start(f32[4,191]{1,0:T(4,128)} %param.9) | copy-start | bytes 9172
  149.3 11.4 %copy-start = (bf16[32,2,16384]{2,1,0:T(2,128)(2,1)}, bf16[32,2,16384]{2,1,0:T(2,128)(2,1)S(1)}, u32[]{:S(2)}) copy-start(bf16[32,2,16384]{2,1,0:T(2,128)(2,1)S(1)} %all-to-all-done.1) | copy-start | bytes 6291460
  149.3 104.5 %all-to-all-start.6 = ((bf16[32,2,16384]{2,1,0:T(2,128)(2,1)}), bf16[32,2,16384]{2,1,0:T(2,128)(2,1)}, u32[]{:S(2)}, u32[]{:S(2)}) async-start(bf16[32,2,16384]{2,1,0:T(2,128)(2,1)} %reshape.687), calls=%async_computation.6 | async-start | bytes 4194304 | tf_op jit(solution)/shard_map/all_to_all | solution.py:106
  179.1 0.8 copy-start.4
  253.8 18.5 %all-to-all-start.2 = ((f32[32,1,256]{2,1,0:T(1,128)}), f32[32,1,256]{2,1,0:T(1,128)S(1)}, u32[]{:S(2)}, u32[]{:S(2)}) async-start(f32[32,1,256]{2,1,0:T(1,128)} %copy.162), calls=%async_computation.2 | async-start | bytes 65536 | tf_op jit(solution)/shard_map/all_to_all | solution.py:135
  272.3 19.4 %all-to-all-start.4 = ((f32[32,1,256]{2,1,0:T(1,128)}), f32[32,1,256]{2,1,0:T(1,128)S(1)}, u32[]{:S(2)}, u32[]{:S(2)}) async-start(f32[32,1,256]{2,1,0:T(1,128)} %copy.171), calls=%async_computation.4 | async-start | bytes 65536 | tf_op jit(solution)/shard_map/all_to_all | solution.py:136
  291.7 193.0 %all-to-all-start.3 = ((f32[32,1,32768]{2,1,0:T(1,128)}), f32[32,1,32768]{2,1,0:T(1,128)}, u32[]{:S(2)}, u32[]{:S(2)}) async-start(f32[32,1,32768]{2,1,0:T(1,128)} %copy.168), calls=%async_computation.3 | async-start | bytes 8388608 | tf_op jit(solution)/shard_map/all_to_all | solution.py:134
  506.6 23.9 %all-to-all-start.5 = ((f32[32,1,512]{2,1,0:T(1,128)}), f32[32,1,512]{2,1,0:T(1,128)S(1)}, u32[]{:S(2)}, u32[]{:S(2)}) async-start(f32[32,1,512]{2,1,0:T(1,128)} %copy.177), calls=%async_computation.5 | async-start | bytes 131072 | tf_op jit(solution)/shard_map/all_to_all | solution.py:159
  522.0 13.5 %copy-start.1 = (bf16[8,32768]{1,0:T(8,128)(2,1)}, bf16[8,32768]{1,0:T(8,128)(2,1)S(1)}, u32[]{:S(2)}) copy-start(bf16[8,32768]{1,0:T(8,128)(2,1)S(1)} %convolution_convert_fusion.2) | copy-start | bytes 1572868
  531.9 0.8 copy-start.3
  546.4 6.4 copy-start.6
  546.4 254.4 %copy-start.2 = (bf16[8,32768]{1,0:T(8,128)(2,1)S(1)}, bf16[8,32768]{1,0:T(8,128)(2,1)}, u32[]{:S(2)}) copy-start(bf16[8,32768]{1,0:T(8,128)(2,1)} %copy-done.1) | copy-start | bytes 1572868
  546.4 273.8 %all-to-all-start.7 = ((f32[32,1,32768]{2,1,0:T(1,128)}), f32[32,1,32768]{2,1,0:T(1,128)}, u32[]{:S(2)}, u32[]{:S(2)}) async-start(f32[32,1,32768]{2,1,0:T(1,128)} %copy.187), calls=%async_computation.7 | async-start | bytes 8388608 | tf_op jit(solution)/shard_map/all_to_all | solution.py:193
  552.9 173.0 %collective-permute-start.1 = (bf16[64,512]{1,0:T(8,128)(2,1)S(1)}, bf16[64,512]{1,0:T(8,128)(2,1)S(1)}, u32[]{:S(2)}, u32[]{:S(2)}) collective-permute-start(bf16[64,512]{1,0:T(8,128)(2,1)S(1)} %bitcast.224), channel_id=1, source_target_pairs={{0,4},{4,8},{8,12},{12,16},{16,20},{20,24},{24,28},{28,32},{32,36}... | collective-permute-start | bytes 196616 | tf_op jit(solution)/shard_map/ppermute | solution.py:13
  827.6 6.2 collective-permute-start.2
